TPU v7x, 256 devices: a whole 4x4x8 slice. The times are simulated.
256 devices in a mesh: seq: 64 (over x, z, core), mp: 4 (over y).
Axes of the slice: x: 4, y: 4, z: 8, core: 2. Of those that a mesh axis runs over, the one named last changes fastest.
Arguments:
- states: bfloat16 [4, 128, 2560], P(None, 'seq', 'mp'), may hold values from -6 to 6
- norm_gain: float32 [2560], replicated, may hold values from 0.5 to 2
- query_gain: float32 [128], replicated, may hold values from 0.7 to 2
- key_gain: float32 [128], replicated, may hold values from 0.7 to 2
- w_query: bfloat16 [2560, 2048], P(None, 'mp'), may hold values from -0.125 to 0.125
- key_matrix: bfloat16 [2560, 512], P(None, 'mp'), may hold values from -0.125 to 0.125
- value_matrix: bfloat16 [2560, 512], P(None, 'mp'), may hold values from -0.125 to 0.125
- w_out: bfloat16 [2048, 2560], P('mp'), may hold values from -0.125 to 0.125
- cached_key_blocks: bfloat16 [1024, 256, 512], P('seq', None, 'mp'), may hold values from -216 to 216
- cached_value_blocks: bfloat16 [1024, 256, 512], P('seq', None, 'mp'), may hold values from -6 to 6
- req_len: int32 [128], replicated, may hold values from 1 to 16384, as said below
- slot_request: int32 [1024], P('seq'), may hold values from 0 to 127, as said below
- slot_block: int32 [1024], P('seq'), may hold values from 0 to 63
- slot_empty: int32 [1024], P('seq'), may hold values from 0 to 1
Outputs:
- hidden: bfloat16 [4, 128, 2560], P(None, 'seq', 'mp')
- new_keys: bfloat16 [4, 128, 512], P(None, 'seq', 'mp')
- new_values: bfloat16 [4, 128, 512], P(None, 'seq', 'mp')
Inputs may be any that keep to these rules, and one draw needn't show every extreme that they name: `req_len`: exactly 12 requests have length 16384; each other request has length at most 511, and one of them exactly that. Slot s holds positions slot_block[s] * 256 onward of request slot_request[s] unless slot_empty[s] = 1. Each block of a request below its length lies in exactly one slot that is not empty. A request of length 16384 has one block on every index of seq; every block of any other request b lies on index b // 2 of seq.
All inputs are finite; a program needn't handle non-finite values.
Results may differ from a plain program's by a relative error of at most 0.0098.
Values may be sent and summed in bfloat16 or wider, within the bound.
No kernel may reach another device: no remote copies, remote signals or barrier semaphores. Data moves between devices by JAX's collectives and lax.ppermute only.
A program may use at most 64 MiB of HBM per device.

v0:
```python
import jax
import jax.numpy as jnp
from jax import lax
from jax.sharding import PartitionSpec as P

HEAD_SIZE = 128
STEPS = 4
ROPE_BASE = 1000000.0
NEGATIVE = -1e30
HIGHEST = lax.Precision.HIGHEST


def scaled_rms(values, gain):
    return values * lax.rsqrt(jnp.mean(values * values, axis=-1, keepdims=True) + 1e-06) * gain


def rotate(values, positions):
    halfway = values.shape[-1] // 2
    frequency = ROPE_BASE ** (-(jnp.arange(halfway, dtype=jnp.float32) * 2.0) / values.shape[-1])
    angles = positions.astype(jnp.float32)[..., None, None] * frequency
    cosine = jnp.cos(angles)
    sine_part = jnp.sin(angles)
    leading = values[..., :halfway]
    trailing = values[..., halfway:]
    return jnp.concatenate(
        [leading * cosine - trailing * sine_part, trailing * cosine + leading * sine_part], axis=-1
    )


def project(inputs, positions, norm_gain, query_gain, key_gain, w_query, key_matrix, value_matrix):
    number = inputs.shape[0]
    normed = scaled_rms(inputs.astype(jnp.float32), norm_gain).astype(jnp.bfloat16)
    query_rows = jnp.dot(normed, w_query, preferred_element_type=jnp.float32).reshape(
        number, -1, HEAD_SIZE
    )
    keys = jnp.dot(normed, key_matrix, preferred_element_type=jnp.float32).reshape(
        number, -1, HEAD_SIZE
    )
    values = jnp.dot(normed, value_matrix, preferred_element_type=jnp.float32).astype(jnp.bfloat16)
    query_rows = (
        rotate(scaled_rms(query_rows, query_gain), positions)
        .reshape(number, -1)
        .astype(jnp.bfloat16)
    )
    keys = rotate(scaled_rms(keys, key_gain), positions).reshape(number, -1).astype(jnp.bfloat16)
    return (query_rows, keys, values)


def shards(
    states,
    norm_gain,
    query_gain,
    key_gain,
    w_query,
    key_matrix,
    value_matrix,
    w_out,
    cached_key_blocks,
    cached_value_blocks,
    req_len,
    slot_request,
    slot_block,
    slot_empty,
):
    own_rows = states.shape[1]
    first_row = lax.axis_index("seq") * own_rows
    kv_heads = key_matrix.shape[1] // HEAD_SIZE
    q_heads = w_query.shape[1] // HEAD_SIZE
    head_sharing = q_heads // kv_heads
    query_width = w_query.shape[1]
    kv_width = key_matrix.shape[1]
    slot_count = cached_key_blocks.shape[0]
    block_len = cached_key_blocks.shape[1]
    requests = req_len.shape[0]
    scaling = HEAD_SIZE ** (-0.5)
    slot_len = jnp.take(req_len, slot_request)
    offsets = jnp.arange(block_len, dtype=jnp.int32)
    filled = (slot_empty[:, None] == 0) & (
        slot_block[:, None] * block_len + offsets[None, :] < slot_len[:, None]
    )
    filled_wide = filled[None, :, None, None, :]
    belongs = (slot_request[None, :] == jnp.arange(requests, dtype=jnp.int32)[:, None]) & (
        slot_empty[None, :] == 0
    )
    belongs_float = belongs.astype(jnp.float32)
    keys_split = cached_key_blocks.reshape(slot_count, block_len, kv_heads, HEAD_SIZE)
    values_split = cached_value_blocks.reshape(slot_count, block_len, kv_heads, HEAD_SIZE)
    turn_spans = [(sequence_index, sequence_index + 1) for sequence_index in range(STEPS)]
    past_keys = []
    past_values = []
    results = []
    for low_turn, high_turn in turn_spans:
        number = high_turn - low_turn
        turn_ids = jnp.arange(low_turn, high_turn, dtype=jnp.int32)
        block_states = states[low_turn:high_turn]
        wide_states = lax.all_gather(block_states, "mp", axis=2, tiled=True)
        portion = lax.all_gather(wide_states, "seq", axis=1, tiled=True)
        portion_rows = portion.shape[1]
        portion_positions = req_len[None, :] + turn_ids[:, None]
        part_query, part_key, part_value = project(
            portion.reshape(number * portion_rows, -1),
            portion_positions.reshape(-1),
            norm_gain,
            query_gain,
            key_gain,
            w_query,
            key_matrix,
            value_matrix,
        )
        everyone = jnp.concatenate([part_query, part_key, part_value], axis=1).reshape(
            number, portion_rows, -1
        )
        own_packed = lax.dynamic_slice_in_dim(everyone, first_row, own_rows, 1)
        all_query = everyone[:, :, :query_width]
        own_heads = own_packed[:, :, :query_width].reshape(
            number, own_rows, kv_heads, head_sharing, HEAD_SIZE
        )
        past_keys.append(own_packed[:, :, query_width : query_width + kv_width])
        past_values.append(own_packed[:, :, query_width + kv_width :])
        slot_query = jnp.take(all_query, slot_request, axis=1).reshape(
            number, slot_count, kv_heads, head_sharing, HEAD_SIZE
        )
        scores = (
            jnp.einsum(
                "tsngd,sknd->tsngk", slot_query, keys_split, preferred_element_type=jnp.float32
            )
            * scaling
        )
        slot_maximum = jnp.max(jnp.where(filled_wide, scores, NEGATIVE), axis=-1)
        row_top = jnp.max(
            jnp.where(belongs[None, :, :, None, None], slot_maximum[:, None], NEGATIVE), axis=2
        )
        slot_reference = jnp.take(row_top, slot_request, axis=1)
        weights = jnp.where(
            filled_wide,
            jnp.exp(jnp.where(filled_wide, scores - slot_reference[..., None], 0.0)),
            0.0,
        )
        slot_total = jnp.sum(weights, axis=-1)
        slot_mix = jnp.einsum(
            "tsngk,sknd->tsngd",
            weights.astype(jnp.bfloat16),
            values_split,
            preferred_element_type=jnp.float32,
        )
        row_total = jnp.einsum("bs,tsng->tbng", belongs_float, slot_total, precision=HIGHEST)
        row_mix = jnp.einsum("bs,tsngd->tbngd", belongs_float, slot_mix, precision=HIGHEST)
        every_top = lax.pmax(row_top, "seq")
        every_factor = jnp.exp(row_top - every_top)
        summed_total, summed_mix = lax.psum(
            (row_total * every_factor, row_mix * every_factor[..., None]), "seq"
        )
        own_top = lax.dynamic_slice_in_dim(every_top, first_row, own_rows, 1)
        own_total = lax.dynamic_slice_in_dim(summed_total, first_row, own_rows, 1)
        own_mix = lax.dynamic_slice_in_dim(summed_mix, first_row, own_rows, 1)
        earlier_keys = jnp.concatenate(past_keys, axis=0).reshape(
            high_turn, own_rows, kv_heads, HEAD_SIZE
        )
        earlier_values = jnp.concatenate(past_values, axis=0).reshape(
            high_turn, own_rows, kv_heads, HEAD_SIZE
        )
        fresh_scores = (
            jnp.einsum(
                "trngd,jrnd->trngj", own_heads, earlier_keys, preferred_element_type=jnp.float32
            )
            * scaling
        )
        allowed = (jnp.arange(high_turn, dtype=jnp.int32)[None, :] <= turn_ids[:, None])[
            :, None, None, None, :
        ]
        fresh_top = jnp.max(jnp.where(allowed, fresh_scores, NEGATIVE), axis=-1)
        overall = jnp.maximum(own_top, fresh_top)
        retained = jnp.exp(own_top - overall)
        fresh_weights = jnp.where(
            allowed, jnp.exp(jnp.where(allowed, fresh_scores - overall[..., None], 0.0)), 0.0
        )
        denominator = own_total * retained + jnp.sum(fresh_weights, axis=-1)
        mixture = own_mix * retained[..., None] + jnp.einsum(
            "trngj,jrnd->trngd",
            fresh_weights.astype(jnp.bfloat16),
            earlier_values,
            preferred_element_type=jnp.float32,
        )
        attended = (
            (mixture / denominator[..., None])
            .astype(jnp.bfloat16)
            .reshape(number * own_rows, query_width)
        )
        projected_out = jnp.dot(attended, w_out, preferred_element_type=jnp.float32).reshape(
            number, own_rows, -1
        )
        summed = lax.psum_scatter(projected_out, "mp", scatter_dimension=2, tiled=True)
        results.append((block_states.astype(jnp.float32) + summed).astype(jnp.bfloat16))
    return (
        jnp.concatenate(results, axis=0),
        jnp.concatenate(past_keys, axis=0),
        jnp.concatenate(past_values, axis=0),
    )


def solution(mesh):
    placed = (
        P(None, "seq", "mp"),
        P(),
        P(),
        P(),
        P(None, "mp"),
        P(None, "mp"),
        P(None, "mp"),
        P("mp", None),
        P("seq", None, "mp"),
        P("seq", None, "mp"),
        P(),
        P("seq"),
        P("seq"),
        P("seq"),
    )
    return jax.shard_map(
        shards,
        mesh=mesh,
        in_specs=placed,
        out_specs=(P(None, "seq", "mp"), P(None, "seq", "mp"), P(None, "seq", "mp")),
        check_vma=False,
    )
```

profile of v0, /device:TPU:2, one launch (start us, length us, event | category | flops | bytes accessed | tf_op | source)
XLA Modules:
  0.0 764.8 jit_solution(867895954115995821)
XLA Ops:
  8.8 12.3 %all_gather.28 = bf16[1,2,2560]{2,0,1:T(2,128)(2,1)S(1)} all-gather(bf16[1,2,640]{2,0,1:T(2,128)(2,1)S(1)} %copy.475), channel_id=1, replica_groups=mesh['seq'=64,'mp'=4] {'mp'}, dimensions={2}, use_global_device_ids=true | all-gather | bytes 12800 | tf_op jit(solution)/shard_map/all_gather | solution.py:96
  21.1 11.8 %all_gather.24 = bf16[1,2,2560]{2,0,1:T(2,128)(2,1)S(1)} all-gather(bf16[1,2,640]{2,0,1:T(2,128)(2,1)S(1)} %copy.469), channel_id=1, replica_groups=mesh['seq'=64,'mp'=4] {'mp'}, dimensions={2}, use_global_device_ids=true | all-gather | bytes 12800 | tf_op jit(solution)/shard_map/all_gather | solution.py:96
  32.9 53.2 %all_gather.25 = bf16[1,128,2560]{2,0,1:T(2,128)(2,1)S(1)} all-gather(bf16[1,2,2560]{2,0,1:T(2,128)(2,1)S(1)} %all_gather.24), channel_id=1, replica_groups=mesh['seq'=64,'mp'=4] {'seq'}, dimensions={1}, use_global_device_ids=true | all-gather | bytes 665600 | tf_op jit(solution)/shard_map/all_gather | solution.py:97
  86.2 1.3 convert_element_type.197
  87.7 1.3 copy-done.7
  90.1 1.6 multiply_reduce_fusion.7
  91.7 48.7 %all_gather.29 = bf16[1,128,2560]{2,0,1:T(2,128)(2,1)S(1)} all-gather(bf16[1,2,2560]{2,0,1:T(2,128)(2,1)S(1)} %all_gather.28), channel_id=1, replica_groups=mesh['seq'=64,'mp'=4] {'seq'}, dimensions={1}, use_global_device_ids=true | all-gather | bytes 665600 | tf_op jit(solution)/shard_map/all_gather | solution.py:97
  141.7 1.6 multiply_reduce_fusion.5
  143.3 11.8 %all_gather.26 = bf16[1,2,2560]{2,0,1:T(2,128)(2,1)S(1)} all-gather(bf16[1,2,640]{2,0,1:T(2,128)(2,1)S(1)} %copy.472), channel_id=1, replica_groups=mesh['seq'=64,'mp'=4] {'mp'}, dimensions={2}, use_global_device_ids=true | all-gather | bytes 12800 | tf_op jit(solution)/shard_map/all_gather | solution.py:96
  155.1 49.3 %all_gather.27 = bf16[1,128,2560]{2,0,1:T(2,128)(2,1)S(1)} all-gather(bf16[1,2,2560]{2,0,1:T(2,128)(2,1)S(1)} %all_gather.26), channel_id=1, replica_groups=mesh['seq'=64,'mp'=4] {'seq'}, dimensions={1}, use_global_device_ids=true | all-gather | bytes 665600 | tf_op jit(solution)/shard_map/all_gather | solution.py:97
  205.7 1.7 multiply_reduce_fusion.6
  207.4 11.8 %all_gather.30 = bf16[1,2,2560]{2,0,1:T(2,128)(2,1)S(1)} all-gather(bf16[1,2,640]{2,0,1:T(2,128)(2,1)S(1)} %copy.478), channel_id=1, replica_groups=mesh['seq'=64,'mp'=4] {'mp'}, dimensions={2}, use_global_device_ids=true | all-gather | bytes 12800 | tf_op jit(solution)/shard_map/all_gather | solution.py:96
  219.3 48.6 %all_gather.31 = bf16[1,128,2560]{2,0,1:T(2,128)(2,1)S(1)} all-gather(bf16[1,2,2560]{2,0,1:T(2,128)(2,1)S(1)} %all_gather.30), channel_id=1, replica_groups=mesh['seq'=64,'mp'=4] {'seq'}, dimensions={1}, use_global_device_ids=true | all-gather | bytes 665600 | tf_op jit(solution)/shard_map/all_gather | solution.py:97
  269.2 1.6 multiply_reduce_fusion.4
  270.8 4.4 copy.463
  275.3 3.8 multiply_reduce_fusion.3
  279.1 2.2 multiply_reduce_fusion
  281.3 2.2 multiply_reduce_fusion.1
  283.7 1.6 multiply_reduce_fusion.2
  291.8 1.2 multiply_cosine_fusion.7
  295.6 2.0 multiply_multiply_fusion.3
  300.9 1.5 fusion.220
  303.0 1.5 fusion.221
  306.6 1.7 fusion.29
  308.3 1.6 fusion.30
  312.0 109.9 %all-reduce.2 = (f32[1,128,1,4]{1,3,2,0:T(4,128)}, f32[1,128,1,4]{1,3,2,0:T(4,128)}, f32[1,128,1,4]{1,3,2,0:T(4,128)}, f32[1,128,1,4]{1,3,2,0:T(4,128)}) all-reduce(f32[1,128,1,4]{1,3,2,0:T(4,128)} %bitcast.554, f32[1,128,1,4]{1,3,2,0:T(4,128)S(1)} %bitcast.553, ...), channel_id=1, replica_groups=mesh['seq'=64,'mp'=4] {'seq'}, use_global_device_ids=true, to_apply=%region_39.42 | all-reduce | flops 2048 | bytes 16384 | tf_op jit(solution)/shard_map/pmax | solution.py:148
  422.0 1.3 fusion.196
  423.3 1.3 fusion.195
  424.5 1.3 fusion.194
  425.8 1.3 fusion.193
  431.2 1.6 fusion.111
  432.8 1.5 fusion.114
  435.1 1.1 fusion.24
  436.2 1.1 fusion.27
  437.3 1.1 fusion.26
  438.5 1.1 fusion.25
  445.7 111.5 %all-reduce = (f32[1,128,1,4]{1,3,2,0:T(4,128)S(1)}, f32[1,128,1,4]{1,3,2,0:T(4,128)S(1)}, f32[1,128,1,4]{1,3,2,0:T(4,128)S(1)}, f32[1,128,1,4]{1,3,2,0:T(4,128)S(1)}) all-reduce(f32[1,128,1,4]{1,3,2,0:T(4,128)S(1)} %fusion.33, f32[1,128,1,4]{1,3,2,0:T(4,128)S(1)} %fusion.34, ...), channel_id=1, replica_groups=mesh['seq'=64,'mp'=4] {'seq'}, use_global_device_ids=true, to_apply=%region_43.46 | all-reduce | flops 2048 | bytes 16384 | tf_op jit(solution)/shard_map/psum | solution.py:150
  559.7 80.1 %all-reduce.5.cloned.1.call-done = (f32[1,128,1,4,128]{1,4,3,2,0:T(8,128)}, f32[1,128,1,4,128]{1,4,3,2,0:T(8,128)}, f32[1,128,1,4,128]{1,4,3,2,0:T(8,128)}, f32[1,128,1,4,128]{1,4,3,2,0:T(8,128)}) async-done(((f32[1,128,1,4,128]{1,4,3,2,0:T(8,128)}, f32[1,128,1,4,128]{1,4,3,2,0:T(8,128)}, f32[1,128,1,4,128]{1,4,3,2,0:T(8,128)}, f32[1,128,1,4,128]{1,4,3,2,0:T(8,128)}), (f32[1,128,1,4,128]{1,4,3,2,0:T(8,128)}, ...) | async-done | bytes 1048592 | tf_op jit(solution)/shard_map/psum | solution.py:150
  640.9 2.2 convolution_bitcast_fusion
  644.2 2.2 convolution_bitcast_fusion.1
  647.5 2.2 convolution_bitcast_fusion.2
  650.8 2.2 convolution_bitcast_fusion.3
  654.2 13.9 %reduce-scatter.19.cloned.1.call-done = f32[640,2]{1,0:T(8,128)} async-done(((f32[2560,2]{1,0:T(8,128)}), f32[640,2]{1,0:T(8,128)}) %reduce-scatter.19.cloned.1.call-update) | async-done | bytes 5136
  669.2 28.5 %reduce-scatter.17.cloned.1.call-done = f32[640,2]{1,0:T(8,128)} async-done(((f32[2560,2]{1,0:T(8,128)}), f32[640,2]{1,0:T(8,128)}) %reduce-scatter.17.cloned.1.call-update) | async-done | bytes 5136
  697.7 1.1 copy.418
  698.8 28.3 %reduce-scatter.15.cloned.1.call-done = f32[640,2]{1,0:T(8,128)} async-done(((f32[2560,2]{1,0:T(8,128)}), f32[640,2]{1,0:T(8,128)}) %reduce-scatter.15.cloned.1.call-update) | async-done | bytes 5136
  728.2 28.3 %reduce-scatter.13.cloned.1.call-done = f32[640,2]{1,0:T(8,128)} async-done(((f32[2560,2]{1,0:T(8,128)}), f32[640,2]{1,0:T(8,128)}) %reduce-scatter.13.cloned.1.call-update) | async-done | bytes 5136
  756.5 1.1 copy.372
  (349 shorter events, 45.1 us)
Async XLA Ops:
  7.2 633.7 %copy-start = (bf16[512,2560]{1,0:T(8,128)(2,1)S(1)}, bf16[512,2560]{1,0:T(8,128)(2,1)}, u32[]{:S(2)}) copy-start(bf16[512,2560]{1,0:T(8,128)(2,1)} %param.25) | copy-start | bytes 7864324
  7.2 632.6 %all-reduce.5.cloned.1.call-start = ((), (), s32[]{:S(2)}) async-start(), calls=%async_computation.8 | async-start | bytes 2097152 | tf_op jit(solution)/shard_map/psum | solution.py:150
  8.7 24.2 %copy-start.34 = (bf16[1,2,640]{2,1,0:T(2,128)(2,1)}, bf16[1,2,640]{2,1,0:T(2,128)(2,1)S(1)}, u32[]{:S(2)}) copy-start(bf16[1,2,640]{2,1,0:T(2,128)(2,1)S(1)} %get-tuple-element.84) | copy-start | bytes 7684
  8.7 24.2 %copy-start.38 = (bf16[1,2,640]{2,1,0:T(2,128)(2,1)}, bf16[1,2,640]{2,1,0:T(2,128)(2,1)S(1)}, u32[]{:S(2)}) copy-start(bf16[1,2,640]{2,1,0:T(2,128)(2,1)S(1)} %get-tuple-element.85) | copy-start | bytes 7684
  8.7 134.6 %copy-start.36 = (bf16[1,2,640]{2,1,0:T(2,128)(2,1)}, bf16[1,2,640]{2,1,0:T(2,128)(2,1)S(1)}, u32[]{:S(2)}) copy-start(bf16[1,2,640]{2,1,0:T(2,128)(2,1)S(1)} %get-tuple-element.86) | copy-start | bytes 7684
  8.7 198.7 %copy-start.40 = (bf16[1,2,640]{2,1,0:T(2,128)(2,1)}, bf16[1,2,640]{2,1,0:T(2,128)(2,1)S(1)}, u32[]{:S(2)}) copy-start(bf16[1,2,640]{2,1,0:T(2,128)(2,1)S(1)} %get-tuple-element.87) | copy-start | bytes 7684
  275.3 3.8 copy-start.5
  275.3 3.8 copy-start.11
  275.3 3.8 copy-start.75
  283.5 4.2 copy-start.16
  283.5 4.9 copy-start.63
  283.5 4.9 copy-start.31
  283.6 5.6 copy-start.67
  283.6 5.6 copy-start.32
  283.6 6.3 copy-start.68
  283.6 6.3 copy-start.33
  283.6 7.1 copy-start.69
  283.6 7.1 copy-start.12
  283.6 7.1 copy-start.22
  283.6 7.1 copy-start.23
  283.6 7.1 copy-start.24
  283.6 7.1 copy-start.62
  285.3 5.5 copy-start.57
  285.3 10.3 %copy-start.60 = (f32[128,4]{0,1:T(4,128)S(1)}, f32[128,4]{0,1:T(4,128)}, u32[]{:S(2)}) copy-start(f32[128,4]{0,1:T(4,128)} %get-tuple-element.150) | copy-start | bytes 6148
  285.3 10.3 %copy-start.59 = (f32[128,4]{0,1:T(4,128)S(1)}, f32[128,4]{0,1:T(4,128)}, u32[]{:S(2)}) copy-start(f32[128,4]{0,1:T(4,128)} %get-tuple-element.152) | copy-start | bytes 6148
  285.3 10.3 %copy-start.55 = (f32[128,4]{0,1:T(4,128)S(1)}, f32[128,4]{0,1:T(4,128)}, u32[]{:S(2)}) copy-start(f32[128,4]{0,1:T(4,128)} %get-tuple-element.146) | copy-start | bytes 6148
  285.3 25.0 %copy-start.45 = (pred[16]{0:T(512)(128)(4,1)}, pred[16]{0:T(512)(128)(4,1)S(1)}, u32[]{:S(2)}) copy-start(pred[16]{0:T(512)(128)(4,1)S(1)} %broadcast_compare_fusion) | copy-start | bytes 52
  286.5 19.3 %copy-start.42 = (s32[1024]{0:T(1024)}, s32[1024]{0:T(1024)S(1)}, u32[]{:S(2)}) copy-start(s32[1024]{0:T(1024)S(1)} %pad_clamp_fusion) | copy-start | bytes 12292
  287.7 18.7 %copy-start.58 = (pred[16]{0:T(512)(128)(4,1)}, pred[16]{0:T(512)(128)(4,1)S(1)}, u32[]{:S(2)}) copy-start(pred[16]{0:T(512)(128)(4,1)S(1)} %get-tuple-element.53) | copy-start | bytes 52
  300.8 4.3 copy-start.18
  300.8 4.3 copy-start.19
  311.4 114.5 %copy-start.25 = (f32[128,4]{0,1:T(4,128)}, f32[128,4]{0,1:T(4,128)S(1)}, u32[]{:S(2)}) copy-start(f32[128,4]{0,1:T(4,128)S(1)} %get-tuple-element.28) | copy-start | bytes 6148
  311.4 114.5 %copy-start.27 = (f32[128,4]{0,1:T(4,128)}, f32[128,4]{0,1:T(4,128)S(1)}, u32[]{:S(2)}) copy-start(f32[128,4]{0,1:T(4,128)S(1)} %get-tuple-element.31) | copy-start | bytes 6148
  436.2 6.7 copy-start.48
  436.2 6.8 copy-start.49
  437.3 6.7 copy-start.47
  437.3 7.2 copy-start.50
  438.5 6.4 copy-start.30
  438.5 6.6 copy-start.28
  438.5 6.8 copy-start.26
  439.6 228.5 %reduce-scatter.19.cloned.1.call-start = ((), (), s32[]{:S(2)}) async-start(), calls=%async_computation.7 | async-start | bytes 1638400
  643.1 54.5 %reduce-scatter.17.cloned.1.call-start = ((), (), s32[]{:S(2)}) async-start(), calls=%async_computation.6 | async-start | bytes 1638400
  646.4 80.6 %reduce-scatter.15.cloned.1.call-start = ((), (), s32[]{:S(2)}) async-start(), calls=%async_computation.5 | async-start | bytes 1638400
  649.7 106.7 %reduce-scatter.13.cloned.1.call-start = ((), (), s32[]{:S(2)}) async-start(), calls=%async_computation.4 | async-start | bytes 1638400
  653.0 104.5 %copy-start.39 = (bf16[1,2,640]{2,1,0:T(2,128)(2,1)S(1)}, bf16[1,2,640]{2,1,0:T(2,128)(2,1)}, u32[]{:S(2)}) copy-start(bf16[1,2,640]{2,1,0:T(2,128)(2,1)} %copy-done.38) | copy-start | bytes 7684
  653.0 104.5 %copy-start.41 = (bf16[1,2,640]{2,1,0:T(2,128)(2,1)S(1)}, bf16[1,2,640]{2,1,0:T(2,128)(2,1)}, u32[]{:S(2)}) copy-start(bf16[1,2,640]{2,1,0:T(2,128)(2,1)} %copy-done.40) | copy-start | bytes 7684
  653.0 104.6 %copy-start.35 = (bf16[1,2,640]{2,1,0:T(2,128)(2,1)S(1)}, bf16[1,2,640]{2,1,0:T(2,128)(2,1)}, u32[]{:S(2)}) copy-start(bf16[1,2,640]{2,1,0:T(2,128)(2,1)} %copy-done.34) | copy-start | bytes 7684
  653.0 104.6 %copy-start.37 = (bf16[1,2,640]{2,1,0:T(2,128)(2,1)S(1)}, bf16[1,2,640]{2,1,0:T(2,128)(2,1)}, u32[]{:S(2)}) copy-start(bf16[1,2,640]{2,1,0:T(2,128)(2,1)} %copy-done.36) | copy-start | bytes 7684
  (33 other events, 69.9 us)
Sparse Core Ops, SparseCore 0:
  439.8 199.9 all-reduce.4
  643.3 24.8 reduce-scatter.18
  670.8 26.7 reduce-scatter.16
  700.2 26.7 reduce-scatter.14
  729.6 26.7 reduce-scatter.12
where the time goes:
time: 766 us; the launch traced here: 765 us
  blocking collectives  469 us (61%)
  waiting for transfers between devices  179 us (23%)
  matrix products  43.9 us (6%)
  local copies, waits for them, and re-layouts  32.9 us (4%)
  other arithmetic  24.7 us (3%)
  between operations  14.9 us (2%)
    all_gather x4, blocking collectives, shards(): portion = lax.all_gather(wide_states, 'seq', axis=1, tiled=True)  200 us
    psum x1, blocking collectives, shards(): lax.psum((row_total * every_factor, row_mix * every_factor[..., None]), '...  112 us
    pmax x1, blocking collectives, shards(): every_top = lax.pmax(row_top, 'seq')  110 us
    unnamed x9, waiting for transfers between devices  99 us
    psum x1, waiting for transfers between devices, shards(): lax.psum((row_total * every_factor, row_mix * every_factor[..., None]), '...  80.1 us
    all_gather x4, blocking collectives, shards(): wide_states = lax.all_gather(block_states, 'mp', axis=2, tiled=True)  47.8 us
  transfers between devices with their start and end apart: 5, of which 5 were waited for; matrix products, arithmetic and copies ran while one was open for 3% of the time, Pallas kernels for 0%

commit v1 on v0

--- a/solution.py
+++ b/solution.py
@@ -94,7 +94,9 @@
         turn_ids = jnp.arange(low_turn, high_turn, dtype=jnp.int32)
         block_states = states[low_turn:high_turn]
         wide_states = lax.all_gather(block_states, "mp", axis=2, tiled=True)
-        portion = lax.all_gather(wide_states, "seq", axis=1, tiled=True)
+        portion = jnp.concatenate(
+            lax.all_to_all(jnp.stack([wide_states] * lax.axis_size("seq")), "seq", 0, 0), axis=1
+        )
         portion_rows = portion.shape[1]
         portion_positions = req_len[None, :] + turn_ids[:, None]
         part_query, part_key, part_value = project(

time: 766 us -> 802 us (1.047); the launches traced: 765 us -> 793 us
  blocking collectives: 469 us -> 270 us
  waiting for transfers between devices: 179 us -> 322 us
  starting transfers between devices: 0.21 us -> 38 us
  local copies, waits for them, and re-layouts: 32.9 us -> 65.9 us
  other arithmetic: 24.7 us -> 39.1 us
    all_gather x4 -> x0, blocking collectives: 200 us -> none  [shards(): portion = lax.all_gather(wide_states, 'seq', axis=1, tiled=True)]
    psum x1, waiting for transfers between devices: 80.1 us -> 211 us  [shards(): lax.psum((row_total * every_factor, row_mix * every_factor[..., None]), '...]
    all_to_all x0 -> x4, starting transfers between devices: none -> 37.1 us  [shards(): lax.all_to_all(jnp.stack([wide_states] * lax.axis_size('seq')), 'seq', 0, 0)]
    convert_element_type x0 -> x8, local copies, waits for them, and re-layouts: none -> 20.9 us  [the longest x4 11.5 us: project(): inputs.astype(jnp.float32)]
    all_to_all x0 -> x4, waiting for transfers between devices: none -> 12.2 us  [shards(): lax.all_to_all(jnp.stack([wide_states] * lax.axis_size('seq')), 'seq', 0, 0)]
  transfers between devices with their start and end apart: 5 -> 9, of which waited for: 5 -> 7; matrix products, arithmetic and copies ran while one was open for 3% -> 6% of each run, Pallas kernels for 0% -> 0%
where the time goes in v1:
time: 802 us; the launch traced here: 793 us
  waiting for transfers between devices  322 us (40%)
  blocking collectives  270 us (34%)
  local copies, waits for them, and re-layouts  65.9 us (8%)
  matrix products  43 us (5%)
  other arithmetic  39.1 us (5%)
  starting transfers between devices  38 us (5%)
  between operations  15.2 us (2%)
    psum x1, waiting for transfers between devices, shards(): lax.psum((row_total * every_factor, row_mix * every_factor[..., None]), '...  211 us
    psum x1, blocking collectives, shards(): lax.psum((row_total * every_factor, row_mix * every_factor[..., None]), '...  113 us
    pmax x1, blocking collectives, shards(): every_top = lax.pmax(row_top, 'seq')  109 us
    unnamed x9, waiting for transfers between devices  98.4 us
    all_gather x4, blocking collectives, shards(): wide_states = lax.all_gather(block_states, 'mp', axis=2, tiled=True)  47.7 us
    all_to_all x4, starting transfers between devices, shards(): lax.all_to_all(jnp.stack([wide_states] * lax.axis_size('seq')), 'seq', 0, 0)  37.1 us
  transfers between devices with their start and end apart: 9, of which 7 were waited for; matrix products, arithmetic and copies ran while one was open for 6% of the time, Pallas kernels for 0%

profile of v1, /device:TPU:2, one launch (start us, length us, event | category | flops | bytes accessed | tf_op | source)
XLA Modules:
  0.0 792.6 jit_solution(7862718056658459816)
XLA Ops:
  8.1 12.3 %all_gather.26 = bf16[1,2,2560]{2,1,0:T(2,128)(2,1)S(1)} all-gather(bf16[1,2,640]{2,1,0:T(2,128)(2,1)S(1)} %get-tuple-element.88), channel_id=1, replica_groups=mesh['seq'=64,'mp'=4] {'mp'}, dimensions={2}, use_global_device_ids=true | all-gather | bytes 12800 | tf_op jit(solution)/shard_map/all_gather | solution.py:96
  21.6 12.0 %all-to-all-start.3 = ((bf16[64,1,2,2560]{3,2,1,0:T(2,128)(2,1)}), bf16[64,1,2,2560]{3,2,1,0:T(2,128)(2,1)S(1)}, u32[]{:S(2)}, u32[]{:S(2)}) async-start(bf16[64,1,2,2560]{3,2,1,0:T(2,128)(2,1)} %stack.11), calls=%async_computation.3 | async-start | bytes 1310720 | tf_op jit(solution)/shard_map/all_to_all | solution.py:98
  33.6 11.9 %all_gather.22 = bf16[1,2,2560]{2,1,0:T(2,128)(2,1)S(1)} all-gather(bf16[1,2,640]{2,1,0:T(2,128)(2,1)S(1)} %get-tuple-element.87), channel_id=1, replica_groups=mesh['seq'=64,'mp'=4] {'mp'}, dimensions={2}, use_global_device_ids=true | all-gather | bytes 12800 | tf_op jit(solution)/shard_map/all_gather | solution.py:96
  45.6 7.3 all-to-all-done.3
  54.0 7.3 all-to-all-start.1
  62.0 11.8 %all_gather.20 = bf16[1,2,2560]{2,1,0:T(2,128)(2,1)S(1)} all-gather(bf16[1,2,640]{2,1,0:T(2,128)(2,1)S(1)} %get-tuple-element.86), channel_id=1, replica_groups=mesh['seq'=64,'mp'=4] {'mp'}, dimensions={2}, use_global_device_ids=true | all-gather | bytes 12800 | tf_op jit(solution)/shard_map/all_gather | solution.py:96
  75.7 4.9 all-to-all-done.1
  81.7 7.3 all-to-all-start
  89.5 4.4 copy.424
  93.9 11.8 %all_gather.24 = bf16[1,2,2560]{2,1,0:T(2,128)(2,1)S(1)} all-gather(bf16[1,2,640]{2,1,0:T(2,128)(2,1)S(1)} %get-tuple-element.89), channel_id=1, replica_groups=mesh['seq'=64,'mp'=4] {'mp'}, dimensions={2}, use_global_device_ids=true | all-gather | bytes 12800 | tf_op jit(solution)/shard_map/all_gather | solution.py:96
  108.3 1.8 multiply_reduce_fusion.2
  111.5 10.5 %all-to-all-start.2 = ((bf16[64,1,2,2560]{3,2,1,0:T(2,128)(2,1)}), bf16[64,1,2,2560]{3,2,1,0:T(2,128)(2,1)}, u32[]{:S(2)}, u32[]{:S(2)}) async-start(bf16[64,1,2,2560]{3,2,1,0:T(2,128)(2,1)} %stack.10), calls=%async_computation.2 | async-start | bytes 1310720 | tf_op jit(solution)/shard_map/all_to_all | solution.py:98
  122.5 1.8 multiply_reduce_fusion.3
  124.5 2.9 reshape.1255
  127.4 2.3 convolution_convert_fusion.3
  129.8 2.9 reshape.1257
  132.6 2.9 reshape.1259
  135.6 2.5 convolution_convert_fusion.2
  141.8 1.6 multiply_reduce_fusion.8
  143.4 1.8 multiply_reduce_fusion.1
  146.0 2.9 reshape.1258
  148.8 2.6 convolution_convert_fusion.1
  151.5 1.6 multiply_reduce_fusion.9
  153.0 5.2 multiply_convert_fusion.7
  158.2 2.7 reshape.1405
  165.2 1.7 fusion.51
  167.6 2.9 reshape.1409
  170.5 2.7 reshape.1410
  174.3 2.9 multiply_reduce_fusion.4
  189.5 1.5 copy.327
  192.4 1.5 copy.326
  193.8 1.5 subtract_convert_fusion.2
  197.0 1.5 copy.347
  205.0 1.7 fusion.5
  206.7 1.6 fusion.6
  213.0 1.6 fusion.58
  214.6 1.5 fusion.61
  218.6 109.1 %all-reduce.2 = (f32[1,128,1,4]{1,3,2,0:T(4,128)S(1)}, f32[1,128,1,4]{1,3,2,0:T(4,128)S(1)}, f32[1,128,1,4]{1,3,2,0:T(4,128)S(1)}, f32[1,128,1,4]{1,3,2,0:T(4,128)S(1)}) all-reduce(f32[1,128,1,4]{1,3,2,0:T(4,128)S(1)} %bitcast.481, f32[1,128,1,4]{1,3,2,0:T(4,128)S(1)} %bitcast.480, ...), channel_id=1, replica_groups=mesh['seq'=64,'mp'=4] {'seq'}, use_global_device_ids=true, to_apply=%region_39.42 | all-reduce | flops 2048 | bytes 16384 | tf_op jit(solution)/shard_map/pmax | solution.py:150
  334.2 112.8 %all-reduce = (f32[1,128,1,4]{1,3,2,0:T(4,128)}, f32[1,128,1,4]{1,3,2,0:T(4,128)}, f32[1,128,1,4]{1,3,2,0:T(4,128)S(1)}, f32[1,128,1,4]{1,3,2,0:T(4,128)S(1)}) all-reduce(f32[1,128,1,4]{1,3,2,0:T(4,128)S(1)} %fusion.9, f32[1,128,1,4]{1,3,2,0:T(4,128)S(1)} %fusion.10, ...), channel_id=1, replica_groups=mesh['seq'=64,'mp'=4] {'seq'}, use_global_device_ids=true, to_apply=%region_43.46 | all-reduce | flops 2048 | bytes 16384 | tf_op jit(solution)/shard_map/psum | solution.py:152
  456.0 211.4 %all-reduce.5.cloned.1.call-done = (f32[1,128,1,4,128]{1,4,3,2,0:T(8,128)}, f32[1,128,1,4,128]{1,4,3,2,0:T(8,128)}, f32[1,128,1,4,128]{1,4,3,2,0:T(8,128)}, f32[1,128,1,4,128]{1,4,3,2,0:T(8,128)}) async-done(((f32[1,128,1,4,128]{1,4,3,2,0:T(8,128)}, f32[1,128,1,4,128]{1,4,3,2,0:T(8,128)}, f32[1,128,1,4,128]{1,4,3,2,0:T(8,128)}, f32[1,128,1,4,128]{1,4,3,2,0:T(8,128)}), (f32[1,128,1,4,128]{1,4,3,2,0:T(8,128)}, ...) | async-done | bytes 1048592 | tf_op jit(solution)/shard_map/psum | solution.py:152
  668.5 2.2 convolution_bitcast_fusion
  671.9 2.2 convolution_bitcast_fusion.1
  675.2 2.2 convolution_bitcast_fusion.2
  678.5 2.2 convolution_bitcast_fusion.3
  682.6 13.2 %reduce-scatter.19.cloned.1.call-done = f32[640,2]{1,0:T(8,128)} async-done(((f32[2560,2]{1,0:T(8,128)}), f32[640,2]{1,0:T(8,128)}) %reduce-scatter.19.cloned.1.call-update) | async-done | bytes 5136
  696.9 28.5 %reduce-scatter.17.cloned.1.call-done = f32[640,2]{1,0:T(8,128)} async-done(((f32[2560,2]{1,0:T(8,128)}), f32[640,2]{1,0:T(8,128)}) %reduce-scatter.17.cloned.1.call-update) | async-done | bytes 5136
  726.4 28.3 %reduce-scatter.15.cloned.1.call-done = f32[640,2]{1,0:T(8,128)} async-done(((f32[2560,2]{1,0:T(8,128)}), f32[640,2]{1,0:T(8,128)}) %reduce-scatter.15.cloned.1.call-update) | async-done | bytes 5136
  755.8 28.3 %reduce-scatter.13.cloned.1.call-done = f32[640,2]{1,0:T(8,128)} async-done(((f32[2560,2]{1,0:T(8,128)}), f32[640,2]{1,0:T(8,128)}) %reduce-scatter.13.cloned.1.call-update) | async-done | bytes 5136
  (372 shorter events, 77.4 us)
Async XLA Ops:
  7.2 661.3 %copy-start = (bf16[512,2560]{1,0:T(8,128)(2,1)S(1)}, bf16[512,2560]{1,0:T(8,128)(2,1)}, u32[]{:S(2)}) copy-start(bf16[512,2560]{1,0:T(8,128)(2,1)} %param.25) | copy-start | bytes 7864324
  7.2 38.3 %copy-start.32 = (s32[16]{0:T(128)S(1)}, s32[16]{0:T(128)}, u32[]{:S(2)}) copy-start(s32[16]{0:T(128)} %param.29) | copy-start | bytes 196
  21.6 31.3 %all-to-all-start.3 = ((bf16[64,1,2,2560]{3,2,1,0:T(2,128)(2,1)}), bf16[64,1,2,2560]{3,2,1,0:T(2,128)(2,1)S(1)}, u32[]{:S(2)}, u32[]{:S(2)}) async-start(bf16[64,1,2,2560]{3,2,1,0:T(2,128)(2,1)} %stack.11), calls=%async_computation.3 | async-start | bytes 1310720 | tf_op jit(solution)/shard_map/all_to_all | solution.py:98
  33.6 27.8 %copy-start.1 = (s32[128]{0:T(128)S(1)}, s32[128]{0:T(128)}, u32[]{:S(2)}) copy-start(s32[128]{0:T(128)} %param.28) | copy-start | bytes 1540
  33.6 40.7 %copy-start.80 = (s32[16]{0:T(128)S(1)}, s32[16]{0:T(128)}, u32[]{:S(2)}) copy-start(s32[16]{0:T(128)} %param.31) | copy-start | bytes 196
  33.6 41.4 %copy-start.71 = (s32[16]{0:T(128)S(1)}, s32[16]{0:T(128)}, u32[]{:S(2)}) copy-start(s32[16]{0:T(128)} %param.30) | copy-start | bytes 196
  45.5 36.2 %copy-start.30 = (s32[1024]{0:T(1024)}, s32[1024]{0:T(1024)S(1)}, u32[]{:S(2)}) copy-start(s32[1024]{0:T(1024)S(1)} %pad_clamp_fusion) | copy-start | bytes 12292
  52.8 54.5 %copy-start.12 = (bf16[64,1,2,2560]{3,2,1,0:T(2,128)(2,1)}, bf16[64,1,2,2560]{3,2,1,0:T(2,128)(2,1)S(1)}, u32[]{:S(2)}) copy-start(bf16[64,1,2,2560]{3,2,1,0:T(2,128)(2,1)S(1)} %all-to-all-done.3) | copy-start | bytes 1966084
  54.0 26.5 %all-to-all-start.1 = ((bf16[64,1,2,2560]{3,2,1,0:T(2,128)(2,1)}), bf16[64,1,2,2560]{3,2,1,0:T(2,128)(2,1)}, u32[]{:S(2)}, u32[]{:S(2)}) async-start(bf16[64,1,2,2560]{3,2,1,0:T(2,128)(2,1)} %stack.9), calls=%async_computation.1 | async-start | bytes 1310720 | tf_op jit(solution)/shard_map/all_to_all | solution.py:98
  61.4 44.8 %copy-start.52 = (f32[64]{0:T(128)}, f32[64]{0:T(128)S(1)}, u32[]{:S(2)}) copy-start(f32[64]{0:T(128)S(1)} %multiply_power_fusion) | copy-start | bytes 772
  74.3 19.6 %copy-start.34 = (pred[16]{0:T(512)(128)(4,1)}, pred[16]{0:T(512)(128)(4,1)S(1)}, u32[]{:S(2)}) copy-start(pred[16]{0:T(512)(128)(4,1)S(1)} %broadcast_compare_fusion) | copy-start | bytes 52
  74.4 31.8 %copy-start.59 = (f32[128]{0:T(128)}, f32[128]{0:T(128)S(1)}, u32[]{:S(2)}) copy-start(f32[128]{0:T(128)S(1)} %get-tuple-element.133) | copy-start | bytes 1540
  74.4 31.8 %copy-start.60 = (f32[128]{0:T(128)}, f32[128]{0:T(128)S(1)}, u32[]{:S(2)}) copy-start(f32[128]{0:T(128)S(1)} %get-tuple-element.132) | copy-start | bytes 1540
  74.4 31.8 %copy-start.62 = (f32[128]{0:T(128)}, f32[128]{0:T(128)S(1)}, u32[]{:S(2)}) copy-start(f32[128]{0:T(128)S(1)} %get-tuple-element.134) | copy-start | bytes 1540
  74.4 31.8 %copy-start.64 = (f32[128]{0:T(128)}, f32[128]{0:T(128)S(1)}, u32[]{:S(2)}) copy-start(f32[128]{0:T(128)S(1)} %get-tuple-element.135) | copy-start | bytes 1540
  81.7 28.6 %all-to-all-start = ((bf16[64,1,2,2560]{3,2,1,0:T(2,128)(2,1)}), bf16[64,1,2,2560]{3,2,1,0:T(2,128)(2,1)}, u32[]{:S(2)}, u32[]{:S(2)}) async-start(bf16[64,1,2,2560]{3,2,1,0:T(2,128)(2,1)} %stack.8), calls=%async_computation | async-start | bytes 1310720 | tf_op jit(solution)/shard_map/all_to_all | solution.py:98
  108.3 29.7 %copy-start.54 = (f32[128]{0:T(128)}, f32[128]{0:T(128)S(1)}, u32[]{:S(2)}) copy-start(f32[128]{0:T(128)S(1)} %rsqrt.126) | copy-start | bytes 1540
  110.3 25.2 %copy-start.56 = (f32[128]{0:T(128)}, f32[128]{0:T(128)S(1)}, u32[]{:S(2)}) copy-start(f32[128]{0:T(128)S(1)} %rsqrt.118) | copy-start | bytes 1540
  111.5 31.9 %all-to-all-start.2 = ((bf16[64,1,2,2560]{3,2,1,0:T(2,128)(2,1)}), bf16[64,1,2,2560]{3,2,1,0:T(2,128)(2,1)}, u32[]{:S(2)}, u32[]{:S(2)}) async-start(bf16[64,1,2,2560]{3,2,1,0:T(2,128)(2,1)} %stack.10), calls=%async_computation.2 | async-start | bytes 1310720 | tf_op jit(solution)/shard_map/all_to_all | solution.py:98
  122.0 5.4 copy-start.10
  122.0 5.4 copy-start.17
  122.0 545.4 %all-reduce.5.cloned.1.call-start = ((), (), s32[]{:S(2)}) async-start(), calls=%async_computation.12 | async-start | bytes 2097152 | tf_op jit(solution)/shard_map/psum | solution.py:152
  158.2 5.6 copy-start.20
  158.2 5.6 copy-start.21
  158.2 7.0 copy-start.53
  158.2 7.0 copy-start.61
  158.2 7.0 copy-start.63
  174.3 3.0 copy-start.16
  182.8 12.6 %copy-start.37 = (bf16[1,2,768]{2,1,0:T(2,128)(2,1)}, bf16[1,2,768]{2,1,0:T(2,128)(2,1)S(1)}, u32[]{:S(2)}) copy-start(bf16[1,2,768]{2,1,0:T(2,128)(2,1)S(1)} %fusion.90) | copy-start | bytes 9220
  189.0 11.2 %copy-start.38 = (bf16[1,2,768]{2,1,0:T(2,128)(2,1)}, bf16[1,2,768]{2,1,0:T(2,128)(2,1)S(1)}, u32[]{:S(2)}) copy-start(bf16[1,2,768]{2,1,0:T(2,128)(2,1)S(1)} %fusion.91) | copy-start | bytes 9220
  195.4 4.8 copy-start.18
  195.4 4.8 copy-start.19
  195.4 6.3 copy-start.31
  196.4 7.2 copy-start.39
  201.1 5.6 copy-start.40
  205.0 3.3 copy-start.3
  208.3 4.4 copy-start.65
  213.0 3.2 copy-start.4
  216.6 116.7 %copy-start.33 = (s32[16]{0:T(128)S(1)}, s32[16]{0:T(128)}, u32[]{:S(2)}) copy-start(s32[16]{0:T(128)} %param.29) | copy-start | bytes 196
  216.6 116.7 %copy-start.35 = (pred[16]{0:T(512)(128)(4,1)S(1)}, pred[16]{0:T(512)(128)(4,1)}, u32[]{:S(2)}) copy-start(pred[16]{0:T(512)(128)(4,1)} %copy-done.34) | copy-start | bytes 52
  332.0 120.8 %copy-start.36 = (f32[1,2,1,4]{1,3,2,0:T(4,128)}, f32[1,2,1,4]{1,3,2,0:T(4,128)S(1)}, u32[]{:S(2)}) copy-start(f32[1,2,1,4]{1,3,2,0:T(4,128)S(1)} %get-tuple-element.49) | copy-start | bytes 100
  450.5 216.9 %copy-start.43 = (f32[2,4]{0,1:T(4,128)S(1)}, f32[2,4]{0,1:T(4,128)}, u32[]{:S(2)}) copy-start(f32[2,4]{0,1:T(4,128)} %get-tuple-element.50) | copy-start | bytes 100
  451.7 3.6 copy-start.68
  452.8 243.0 %reduce-scatter.19.cloned.1.call-start = ((), (), s32[]{:S(2)}) async-start(), calls=%async_computation.11 | async-start | bytes 1638400
  670.8 54.5 %reduce-scatter.17.cloned.1.call-start = ((), (), s32[]{:S(2)}) async-start(), calls=%async_computation.10 | async-start | bytes 1638400
  674.1 80.6 %reduce-scatter.15.cloned.1.call-start = ((), (), s32[]{:S(2)}) async-start(), calls=%async_computation.9 | async-start | bytes 1638400
  677.4 106.7 %reduce-scatter.13.cloned.1.call-start = ((), (), s32[]{:S(2)}) async-start(), calls=%async_computation.8 | async-start | bytes 1638400
  680.7 104.5 %copy-start.29 = (bf16[4,2,640]{2,1,0:T(2,128)(2,1)S(1)}, bf16[4,2,640]{2,1,0:T(2,128)(2,1)}, u32[]{:S(2)}) copy-start(bf16[4,2,640]{2,1,0:T(2,128)(2,1)} %param.18) | copy-start | bytes 30724
  (46 other events, 60.4 us)
Sparse Core Ops, SparseCore 0:
  452.9 214.4 all-reduce.4
  670.9 24.8 reduce-scatter.18
  698.5 26.7 reduce-scatter.16
  727.9 26.7 reduce-scatter.14
  757.3 26.7 reduce-scatter.12
